TPU v7x, 256 devices: a whole 4x4x8 slice. The times are simulated.
256 devices in a mesh: dp: 2 (over y_hi), retr: 16 (over x, y_lo, core), tensor: 8 (over z).
Axes of the slice: x: 4, y: 4 (y_hi: 2, y_lo: 2; y = y_hi * 2 + y_lo), z: 8, core: 2. Of those that a mesh axis runs over, the one named last changes fastest.
Arguments:
- hidden_in: bfloat16 [16384, 4096], P(('dp', 'retr'), 'tensor'), may hold values from -12 to 12
- norm_gain: float32 [4096], replicated, may hold values from 0.1 to 1.9
- nbr_table: int32 [256, 2], P(('dp', 'retr')), may hold values from 0 to 63, as said below
- encodings: bfloat16 [64, 128, 1024], P('retr'), may hold values from -21 to 21
- enc_mask: int32 [64, 4], P('retr'), may hold values from 0 to 1, as said below
- w_query: bfloat16 [4096, 4096], P(None, 'tensor'), may hold values from -0.02703125 to 0.02703125
- w_key: bfloat16 [1024, 4096], P(None, 'tensor'), may hold values from -0.1021875 to 0.1021875
- w_value: bfloat16 [1024, 4096], P(None, 'tensor'), may hold values from -0.1875 to 0.1875
- w_out: bfloat16 [4096, 4096], P('tensor'), may hold values from -0.125 to 0.125
Outputs:
- mixed: bfloat16 [16384, 4096], P(('dp', 'retr'), 'tensor')
Inputs may be any that keep to these rules, and one draw needn't show every extreme that they name: `nbr_table`: each aligned block of 8 table rows (the rows of one device) holds 16 distinct ids; at most 2 of them share the value id // 4, and in every block some value of id // 4 has exactly 2. `enc_mask`: in each row the ones come first; the first entry is 1.
All inputs are finite; a program needn't handle non-finite values.
Results may differ from a plain program's by a relative error of at most 0.012.
The roundings to bfloat16 on the way count: a program that leaves them out, or rounds other values in their place, can miss the bound.
Values may be sent and summed in bfloat16 or wider, within the bound.
No kernel may reach another device: no remote copies, remote signals or barrier semaphores. Data moves between devices by JAX's collectives and lax.ppermute only.
A program may use at most 128 MiB of HBM per device.

v0:
```python
import math
import jax
import jax.numpy as jnp
from jax import lax
from jax.sharding import PartitionSpec as P

HD = 128
NBRS = 2
BLOCK = 32


def attend_gathered(queries, key_value, selected_marks, segment_count, head_cols):
    tok_rows = queries.shape[0]
    head_count = head_cols // HD
    entry_keys = key_value.shape[0] // segment_count * key_value.shape[1]
    mask_cols = selected_marks.shape[1]
    key_block = key_value[:, :, :head_cols].reshape(segment_count, entry_keys, head_count, HD)
    value_block = key_value[:, :, head_cols:].reshape(segment_count, entry_keys, head_count, HD)
    key_live = (
        jnp.repeat(selected_marks.reshape(segment_count, NBRS * mask_cols), BLOCK, axis=1) > 0
    )
    query_block = queries.reshape(segment_count, tok_rows // segment_count, head_count, HD)
    factor = 1.0 / math.sqrt(HD)
    scores = (
        jnp.einsum("cqhd,ckhd->chqk", query_block, key_block, preferred_element_type=jnp.float32)
        * factor
    )
    key_open = key_live[:, None, None, :]
    scores = jnp.where(key_open, scores, -1e30)
    row_max = jnp.max(scores, axis=-1, keepdims=True)
    weights = jnp.exp(scores - row_max) * key_open.astype(jnp.float32)
    probabilities = (weights / jnp.sum(weights, axis=-1, keepdims=True)).astype(jnp.bfloat16)
    attended = jnp.einsum(
        "chqk,ckhd->cqhd", probabilities, value_block, preferred_element_type=jnp.float32
    )
    return attended.astype(jnp.bfloat16).reshape(tok_rows, head_cols)


def local(hidden_in, norm_gain, nbr_table, encodings, enc_mask, w_query, w_key, w_value, w_out):
    gathered = lax.all_gather(hidden_in, "tensor", axis=1, tiled=True)
    widened = gathered.astype(jnp.float32)
    mean_sq = jnp.mean(widened * widened, axis=-1, keepdims=True)
    normed = (widened * lax.rsqrt(mean_sq + 1e-05) * norm_gain).astype(jnp.bfloat16)
    queries = jnp.dot(normed, w_query, preferred_element_type=jnp.float32).astype(jnp.bfloat16)
    w_both = jnp.concatenate([w_key, w_value], axis=1)
    segment_count = nbr_table.shape[0]
    entry_len = encodings.shape[1]
    enc_width = encodings.shape[2]
    head_cols = w_key.shape[1]
    wanted = nbr_table.reshape(-1)
    need_count = wanted.shape[0]
    live_marks = enc_mask.astype(jnp.bfloat16)
    entry_rows = lax.all_gather(encodings, "retr", axis=0, tiled=True)
    entry_marks = lax.all_gather(live_marks, "retr", axis=0, tiled=True)
    piece_count = entry_rows.shape[0]
    one_hot = (wanted[:, None] == jnp.arange(piece_count, dtype=jnp.int32)[None, :]).astype(
        jnp.bfloat16
    )
    picked = jnp.einsum(
        "jn,nre->jre", one_hot, entry_rows, preferred_element_type=jnp.float32
    ).astype(jnp.bfloat16)
    picked_marks = jnp.dot(one_hot, entry_marks, preferred_element_type=jnp.float32).astype(
        jnp.bfloat16
    )
    key_value = jnp.dot(
        picked.reshape(need_count * entry_len, enc_width),
        w_both,
        preferred_element_type=jnp.float32,
    )
    key_value = key_value.astype(jnp.bfloat16).reshape(need_count, entry_len, 2 * head_cols)
    attended = attend_gathered(queries, key_value, picked_marks, segment_count, head_cols)
    partial_value = jnp.dot(attended, w_out, preferred_element_type=jnp.float32)
    summed = lax.psum_scatter(partial_value, "tensor", scatter_dimension=1, tiled=True)
    return (hidden_in.astype(jnp.float32) + summed).astype(jnp.bfloat16)


def solution(mesh):
    in_specs = (
        P(("dp", "retr"), "tensor"),
        P(),
        P(("dp", "retr"), None),
        P("retr", None, None),
        P("retr", None),
        P(None, "tensor"),
        P(None, "tensor"),
        P(None, "tensor"),
        P("tensor", None),
    )
    out_specs = P(("dp", "retr"), "tensor")
    return jax.shard_map(local, mesh=mesh, in_specs=in_specs, out_specs=out_specs, check_vma=False)
```

profile of v0, /device:TPU:1, one launch (start us, length us, event | category | flops | bytes accessed | tf_op | source)
XLA Modules:
  0.0 318.5 jit_solution(9526612523659051779)
XLA Ops:
  6.5 0.0 copy-start.6
  6.5 0.0 all-gather.6.cloned.1.call-start
  6.5 0.7 all-gather.6.cloned.1.call-update
  7.3 0.0 all-gather.4.cloned.1.call-start
  7.3 0.7 all-gather.4.cloned.1.call-update
  8.0 0.0 reduce-scatter.2.cloned.1.call-start
  8.1 0.8 copy.24
  8.8 0.1 eq.15
  8.9 0.7 convert_bitcast_fusion
  9.6 21.0 %all-gather = bf16[16,4,4]{2,1,0:T(4,128)(2,1)S(1)} all-gather(bf16[1,4,4]{2,1,0:T(4,128)(2,1)S(1)} %convert_bitcast_fusion), channel_id=1, replica_groups=mesh['dp'=2,'retr'=16,'tensor'=8] {'retr'}, dimensions={0}, use_global_device_ids=true | all-gather | bytes 544 | tf_op jit(solution)/shard_map/all_gather | solution.py:54
  30.6 0.2 fusion.30
  30.8 0.1 copy.28
  30.9 0.1 gt.22
  31.0 0.1 broadcast_in_dim.14
  31.0 0.1 gt.23
  31.2 36.4 %all-gather.6.cloned.1.call-done = bf16[512,4096]{1,0:T(8,128)(2,1)} async-done(((bf16[512,512]{1,0:T(8,128)(2,1)}), bf16[512,4096]{1,0:T(8,128)(2,1)}) %all-gather.6.cloned.1.call-update) | async-done | bytes 4194320 | tf_op jit(solution)/shard_map/all_gather | solution.py:40
  67.5 0.0 copy-start.1
  67.5 3.2 %fusion.3 = f32[512]{0:T(512)S(1)} fusion(bf16[512,4096]{1,0:T(8,128)(2,1)} %all-gather.6.cloned.1.call-done), kind=kLoop, calls=%fused_computation.5 | loop fusion | flops 6290944 | bytes 4196352 | tf_op jit(solution)/shard_map/reduce_sum | solution.py:42
  70.8 0.0 copy-done.6
  70.8 0.2 copy-done.1
  71.0 4.6 %fusion.24 = bf16[512,512]{1,0:T(8,128)(2,1)S(1)} fusion(bf16[4096,512]{1,0:T(8,128)(2,1)} %param.14, bf16[512,4096]{1,0:T(8,128)(2,1)S(1)} %copy-done.1, f32[4096]{0:T(1024)S(1)} %copy-done.6, f32[512]{0:T(512)S(1)} %add_rsqrt_fusion), kind=kOutput, calls=%fused_computation.25 | convolution fusion | flops 2156134400 | bytes 8931328 | tf_op jit(solution)/shard_map/dot_general | solution.py:44
  75.6 0.1 reshape.49
  75.7 87.0 %all-gather.4.cloned.1.call-done = bf16[64,128,1024]{2,1,0:T(8,128)(2,1)} async-done(((bf16[4,128,1024]{2,1,0:T(8,128)(2,1)}), bf16[64,128,1024]{2,1,0:T(8,128)(2,1)}) %all-gather.4.cloned.1.call-update) | async-done | bytes 16777232 | tf_op jit(solution)/shard_map/all_gather | solution.py:53
  162.7 23.7 %fusion.10 = bf16[16,128,1024]{2,0,1:T(8,128)(2,1)S(1)} fusion(bf16[64,128,1024]{2,1,0:T(8,128)(2,1)} %all-gather.4.cloned.1.call-done, s32[16]{0:T(128)S(1)} %eq.15), kind=kOutput, calls=%fused_computation.12 | convolution fusion | flops 270533632 | bytes 20971584 | tf_op jit(solution)/shard_map/jn,nre->jre/dot_general | solution.py:59
  186.4 0.0 copy-start.4
  186.4 0.0 copy-start.5
  186.4 2.5 copy.26
  188.9 0.0 copy-done.4
  189.0 0.0 copy-done.5
  189.0 5.0 %convolution_convert_fusion = bf16[2048,1024]{1,0:T(8,128)(2,1)S(1)} fusion(bf16[2048,1024]{1,0:T(8,128)(2,1)S(1)} %bitcast.20, bf16[1024,512]{1,0:T(8,128)(2,1)S(1)} %copy-done.4, bf16[1024,512]{1,0:T(8,128)(2,1)S(1)} %copy-done.5), kind=kOutput, calls=%fused_computation.11 | convolution fusion | flops 4301258752 | bytes 10485760 | tf_op jit(solution)/shard_map/dot_general | solution.py:65
  194.0 1.8 fusion.46
  195.8 4.0 %reshape.55 = bf16[8,256,4,128]{3,2,1,0:T(4,128)(2,1)} reshape(bf16[16,128,512]{2,1,0:T(8,128)(2,1)} %get-tuple-element.5) | data formatting | bytes 4194304 | tf_op jit(solution)/shard_map/reshape | solution.py:17
  199.8 2.0 reshape.56
  201.8 0.0 copy-start.2
  201.8 4.1 %fusion.47 = (f32[8,4,64]{2,1,0:T(4,128)S(1)}, f32[8,4,64,256]{3,2,1,0:T(8,128)}) fusion(f32[8,256]{1,0:T(8,128)S(1)} %convert_element_type.53, pred[8,256]{1,0:T(8,128)(4,1)S(1)} %gt.23, bf16[8,256,4,128]{3,2,1,0:T(4,128)(2,1)} %reshape.55, bf16[8,64,4,128]{3,2,1,0:T(4,128)(2,1)S(1)} %reshape.49), kind=kOutput, calls=%fused_computation.48 | convolution fusion | flops 136839424 | bytes 4737024 | tf_op jit(solution)/shard_map/sub | solution.py:31
  206.0 0.0 copy-done.2
  206.0 0.0 copy-start
  206.0 2.3 fusion.27
  208.3 0.4 copy.33
  208.7 0.1 copy-done
  208.8 5.6 %fusion.35 = f32[512,4096]{1,0:T(8,128)} fusion(bf16[512,4096]{1,0:T(8,128)(2,1)S(1)} %copy-done, bf16[64,8,4,128]{3,2,1,0:T(4,128)(2,1)S(1)} %bitcast.21), kind=kOutput, calls=%fused_computation.34 | convolution fusion | flops 2147483648 | bytes 13107200 | tf_op jit(solution)/shard_map/dot_general | solution.py:72
  214.4 0.0 copy-start.3
  214.4 0.0 reduce-scatter.2.cloned.1.call-update
  214.4 95.4 %reduce-scatter.2.cloned.1.call-done = f32[512,512]{1,0:T(8,128)} async-done(((f32[512,4096]{1,0:T(8,128)}), f32[512,512]{1,0:T(8,128)}) %reduce-scatter.2.cloned.1.call-update) | async-done | bytes 1048592 | tf_op jit(solution)/shard_map/reduce_scatter | solution.py:73
  309.8 0.0 copy-done.3
  309.8 2.2 add_convert_fusion
  (2 shorter events, 0.0 us)
Async XLA Ops:
  6.5 64.2 %copy-start.6 = (f32[4096]{0:T(1024)S(1)}, f32[4096]{0:T(1024)}, u32[]{:S(2)}) copy-start(f32[4096]{0:T(1024)} %param.10) | copy-start | bytes 49156
  6.5 61.0 %all-gather.6.cloned.1.call-start = ((), (), s32[]{:S(2)}) async-start(), calls=%async_computation.2 | async-start | bytes 4718592 | tf_op jit(solution)/shard_map/all_gather | solution.py:40
  7.3 155.4 %all-gather.4.cloned.1.call-start = ((), (), s32[]{:S(2)}) async-start(), calls=%async_computation.1 | async-start | bytes 17825792 | tf_op jit(solution)/shard_map/all_gather | solution.py:53
  8.0 301.8 %reduce-scatter.2.cloned.1.call-start = ((), (), s32[]{:S(2)}) async-start(), calls=%async_computation.3 | async-start | bytes 9437184 | tf_op jit(solution)/shard_map/reduce_scatter | solution.py:73
  67.5 3.4 %copy-start.1 = (bf16[512,4096]{1,0:T(8,128)(2,1)S(1)}, bf16[512,4096]{1,0:T(8,128)(2,1)}, u32[]{:S(2)}) copy-start(bf16[512,4096]{1,0:T(8,128)(2,1)} %all-gather.6.cloned.1.call-done) | copy-start | bytes 12582916
  186.4 2.6 copy-start.4
  186.4 2.6 copy-start.5
  201.8 4.2 %copy-start.2 = (bf16[8,256,4,128]{3,2,1,0:T(4,128)(2,1)S(1)}, bf16[8,256,4,128]{3,2,1,0:T(4,128)(2,1)}, u32[]{:S(2)}) copy-start(bf16[8,256,4,128]{3,2,1,0:T(4,128)(2,1)} %reshape.56) | copy-start | bytes 6291460
  206.0 2.8 copy-start
  214.4 95.4 %copy-start.3 = (bf16[512,512]{1,0:T(8,128)(2,1)S(1)}, bf16[512,512]{1,0:T(8,128)(2,1)}, u32[]{:S(2)}) copy-start(bf16[512,512]{1,0:T(8,128)(2,1)} %param.9) | copy-start | bytes 1572868
Sparse Core Ops, SparseCore 0:
  9.1 58.3 all-gather.5
  69.4 93.2 all-gather.3
  214.5 95.2 reduce-scatter.1
where the time goes:
time: 319 us
  waiting for transfers between devices  220 us (69%)
  matrix products  45.5 us (14%)
  blocking collectives  21 us (7%)
  between operations  13.2 us (4%)
  local copies, waits for them, and re-layouts  12.5 us (4%)
  other arithmetic  6.11 us (2%)
    reduce_scatter x1, waiting for transfers between devices, local(): lax.psum_scatter(partial_value, 'tensor', scatter_dimension=1, tiled=True)  95.4 us
    all_gather x1, waiting for transfers between devices, local(): entry_rows = lax.all_gather(encodings, 'retr', axis=0, tiled=True)  87 us
    all_gather x1, waiting for transfers between devices, local(): gathered = lax.all_gather(hidden_in, 'tensor', axis=1, tiled=True)  36.4 us
    dot_general x1, matrix products, local(): jnp.einsum('jn,nre->jre', one_hot, entry_rows, preferred_element_type=jnp...  23.7 us
    all_gather x1, blocking collectives, local(): entry_marks = lax.all_gather(live_marks, 'retr', axis=0, tiled=True)  21 us
  transfers between devices with their start and end apart: 3, of which 3 were waited for; matrix products, arithmetic and copies ran while one was open for 3% of the time, Pallas kernels for 0%

commit v1 on v0

--- a/solution.py
+++ b/solution.py
@@ -7,6 +7,24 @@
 HD = 128
 NBRS = 2
 BLOCK = 32
+
+
+def collect(value, axis, dim):
+    ways, here, step = (lax.axis_size(axis), lax.axis_index(axis), value.shape[dim])
+    dims = [n * ways if d == dim else n for d, n in enumerate(value.shape)]
+    full = lax.dynamic_update_slice_in_dim(
+        jnp.zeros(dims, value.dtype), value, here * step, axis=dim
+    )
+    going_up = going_down = value
+    for far in range(1, ways // 2 + 1):
+        going_up = lax.ppermute(going_up, axis, [(d, (d + 1) % ways) for d in range(ways)])
+        full = lax.dynamic_update_slice_in_dim(full, going_up, (here - far) % ways * step, axis=dim)
+        if 2 * far < ways:
+            going_down = lax.ppermute(going_down, axis, [(d, (d - 1) % ways) for d in range(ways)])
+            full = lax.dynamic_update_slice_in_dim(
+                full, going_down, (here + far) % ways * step, axis=dim
+            )
+    return full
 
 
 def attend_gathered(queries, key_value, selected_marks, segment_count, head_cols):
@@ -37,7 +55,7 @@
 
 
 def local(hidden_in, norm_gain, nbr_table, encodings, enc_mask, w_query, w_key, w_value, w_out):
-    gathered = lax.all_gather(hidden_in, "tensor", axis=1, tiled=True)
+    gathered = collect(hidden_in, "tensor", 1)
     widened = gathered.astype(jnp.float32)
     mean_sq = jnp.mean(widened * widened, axis=-1, keepdims=True)
     normed = (widened * lax.rsqrt(mean_sq + 1e-05) * norm_gain).astype(jnp.bfloat16)

time: 319 us -> 269 us (0.84); the launches traced: 319 us -> 264 us
  waiting for transfers between devices: 220 us -> 155 us
  starting transfers between devices: 0.08 us -> 12.9 us
    all_gather x1, waiting for transfers between devices: 87 us -> 22.8 us  [local(): entry_rows = lax.all_gather(encodings, 'retr', axis=0, tiled=True)]
    all_gather x1 -> x0, waiting for transfers between devices: 36.4 us -> none  [local(): gathered = lax.all_gather(hidden_in, 'tensor', axis=1, tiled=True)]
    ppermute x0 -> x7, waiting for transfers between devices: none -> 36.4 us  [the longest x4 26.2 us: collect(): lax.ppermute(going_up, axis, [(d, (d + 1) % ways) for d in range(ways)])]
    ppermute x0 -> x7, starting transfers between devices: none -> 12.8 us  [the longest x3 9.73 us: collect(): lax.ppermute(going_down, axis, [(d, (d - 1) % ways) for d in range(ways)])]
  transfers between devices with their start and end apart: 3 -> 9, of which waited for: 3 -> 6; matrix products, arithmetic and copies ran while one was open for 3% -> 2% of each run, Pallas kernels for 0% -> 0%
where the time goes in v1:
time: 269 us; the launch traced here: 264 us
  waiting for transfers between devices  155 us (58%)
  matrix products  43.4 us (16%)
  blocking collectives  21.6 us (8%)
  between operations  13.9 us (5%)
  local copies, waits for them, and re-layouts  13.3 us (5%)
  starting transfers between devices  12.9 us (5%)
  other arithmetic  3.77 us (1%)
    reduce_scatter x1, waiting for transfers between devices, local(): lax.psum_scatter(partial_value, 'tensor', scatter_dimension=1, tiled=True)  95.3 us
    ppermute x4, waiting for transfers between devices, collect(): lax.ppermute(going_up, axis, [(d, (d + 1) % ways) for d in range(ways)])  26.2 us
    dot_general x1, matrix products, local(): jnp.einsum('jn,nre->jre', one_hot, entry_rows, preferred_element_type=jnp...  23.7 us
    all_gather x1, waiting for transfers between devices, local(): entry_rows = lax.all_gather(encodings, 'retr', axis=0, tiled=True)  22.8 us
    all_gather x1, blocking collectives, local(): entry_marks = lax.all_gather(live_marks, 'retr', axis=0, tiled=True)  21.6 us
    ppermute x3, waiting for transfers between devices, collect(): lax.ppermute(going_down, axis, [(d, (d - 1) % ways) for d in range(ways)])  10.2 us
    ppermute x3, starting transfers between devices, collect(): lax.ppermute(going_down, axis, [(d, (d - 1) % ways) for d in range(ways)])  9.73 us
    dot_general x1, matrix products, local(): partial_value = jnp.dot(attended, w_out, preferred_element_type=jnp.float32)  5.58 us
  transfers between devices with their start and end apart: 9, of which 6 were waited for; matrix products, arithmetic and copies ran while one was open for 2% of the time, Pallas kernels for 0%

profile of v1, /device:TPU:1, one launch (start us, length us, event | category | flops | bytes accessed | tf_op | source)
XLA Modules:
  0.0 264.0 jit_solution(16003584664022747254)
XLA Ops:
  6.5 0.7 all-gather.3.cloned.1.call-update
  7.3 0.0 reduce-scatter.2.cloned.1.call-start
  7.3 2.5 collective-permute-start
  9.8 4.0 %collective-permute-start.1 = (bf16[512,512]{1,0:T(8,128)(2,1)}, bf16[512,512]{1,0:T(8,128)(2,1)S(1)}, u32[]{:S(2)}, u32[]{:S(2)}) collective-permute-start(bf16[512,512]{1,0:T(8,128)(2,1)} %param.9), channel_id=1, source_target_pairs={{0,7},{1,0},{2,1},{3,2},{4,3},{5,4},{6,5},{7,6},{8,15},{9,8},{10,9... | collective-permute-start | bytes 1572872 | tf_op jit(solution)/shard_map/ppermute | solution.py:23
  13.9 11.7 %collective-permute-done = bf16[512,512]{1,0:T(8,128)(2,1)S(1)} collective-permute-done((bf16[512,512]{1,0:T(8,128)(2,1)}, bf16[512,512]{1,0:T(8,128)(2,1)S(1)}, u32[]{:S(2)}, u32[]{:S(2)}) %collective-permute-start) | collective-permute-done | bytes 524320 | tf_op jit(solution)/shard_map/ppermute | solution.py:20
  25.6 2.7 %collective-permute-start.3 = (bf16[512,512]{1,0:T(8,128)(2,1)S(1)}, bf16[512,512]{1,0:T(8,128)(2,1)S(1)}, u32[]{:S(2)}, u32[]{:S(2)}) collective-permute-start(bf16[512,512]{1,0:T(8,128)(2,1)S(1)} %collective-permute-done.1), channel_id=1, source_target_pairs={{0,7},{1,0},{2,1},{3,2},{4,3},{5,4},{6,5},{7,6},{8,15},{9,8},{10,9... | collective-permute-start | bytes 1572872 | tf_op jit(solution)/shard_map/ppermute | solution.py:23
  28.3 10.8 %collective-permute-done.2 = bf16[512,512]{1,0:T(8,128)(2,1)S(1)} collective-permute-done((bf16[512,512]{1,0:T(8,128)(2,1)S(1)}, bf16[512,512]{1,0:T(8,128)(2,1)S(1)}, u32[]{:S(2)}, u32[]{:S(2)}) %collective-permute-start.2) | collective-permute-done | bytes 524320 | tf_op jit(solution)/shard_map/ppermute | solution.py:20
  39.1 0.7 convert_bitcast_fusion
  39.7 0.8 copy.24
  40.5 0.1 eq.23
  40.6 21.6 %all-gather = bf16[16,4,4]{2,1,0:T(4,128)(2,1)S(1)} all-gather(bf16[1,4,4]{2,1,0:T(4,128)(2,1)S(1)} %convert_bitcast_fusion), channel_id=1, replica_groups=mesh['dp'=2,'retr'=16,'tensor'=8] {'retr'}, dimensions={0}, use_global_device_ids=true | all-gather | bytes 544 | tf_op jit(solution)/shard_map/all_gather | solution.py:72
  62.2 0.2 fusion.30
  62.4 0.1 copy.28
  62.5 0.1 gt.22
  62.6 0.1 broadcast_in_dim.24
  62.7 0.1 gt.23
  62.8 0.5 broadcast_in_dim.26
  63.3 0.1 constant_dynamic-update-slice_fusion.7
  63.4 3.0 %collective-permute-start.5 = (bf16[512,512]{1,0:T(8,128)(2,1)S(1)}, bf16[512,512]{1,0:T(8,128)(2,1)S(1)}, u32[]{:S(2)}, u32[]{:S(2)}) collective-permute-start(bf16[512,512]{1,0:T(8,128)(2,1)S(1)} %collective-permute-done.3), channel_id=1, source_target_pairs={{0,7},{1,0},{2,1},{3,2},{4,3},{5,4},{6,5},{7,6},{8,15},{9,8},{10,9... | collective-permute-start | bytes 1572872 | tf_op jit(solution)/shard_map/ppermute | solution.py:23
  66.4 0.1 constant_dynamic-update-slice_fusion.6
  66.5 0.5 collective-permute-start.6
  67.1 0.1 constant_dynamic-update-slice_fusion.5
  67.1 0.1 constant_dynamic-update-slice_fusion.4
  67.2 0.0 copy-start.3
  67.3 0.1 constant_dynamic-update-slice_fusion.3
  67.3 0.1 constant_dynamic-update-slice_fusion.2
  67.4 10.1 %collective-permute-done.5 = bf16[512,512]{1,0:T(8,128)(2,1)S(1)} collective-permute-done((bf16[512,512]{1,0:T(8,128)(2,1)S(1)}, bf16[512,512]{1,0:T(8,128)(2,1)S(1)}, u32[]{:S(2)}, u32[]{:S(2)}) %collective-permute-start.5) | collective-permute-done | bytes 524320 | tf_op jit(solution)/shard_map/ppermute | solution.py:23
  77.6 0.1 constant_dynamic-update-slice_fusion.1
  77.6 3.7 %collective-permute-done.6 = bf16[512,512]{1,0:T(8,128)(2,1)S(1)} collective-permute-done((bf16[512,512]{1,0:T(8,128)(2,1)S(1)}, bf16[512,512]{1,0:T(8,128)(2,1)S(1)}, u32[]{:S(2)}, u32[]{:S(2)}) %collective-permute-start.6) | collective-permute-done | bytes 524320 | tf_op jit(solution)/shard_map/ppermute | solution.py:20
  81.3 0.1 constant_dynamic-update-slice_fusion
  81.4 0.9 fusion.3
  82.3 2.5 fusion.24
  84.8 0.1 reshape.49
  84.9 22.8 %all-gather.3.cloned.1.call-done = bf16[64,128,1024]{2,1,0:T(8,128)(2,1)} async-done(((bf16[4,128,1024]{2,1,0:T(8,128)(2,1)}), bf16[64,128,1024]{2,1,0:T(8,128)(2,1)}) %all-gather.3.cloned.1.call-update) | async-done | bytes 16777232 | tf_op jit(solution)/shard_map/all_gather | solution.py:71
  107.7 23.7 %fusion.10 = bf16[16,128,1024]{2,0,1:T(8,128)(2,1)S(1)} fusion(bf16[64,128,1024]{2,1,0:T(8,128)(2,1)} %all-gather.3.cloned.1.call-done, s32[16]{0:T(128)S(1)} %eq.23), kind=kOutput, calls=%fused_computation.12 | convolution fusion | flops 270533632 | bytes 20971584 | tf_op jit(solution)/shard_map/jn,nre->jre/dot_general | solution.py:77
  131.4 2.5 copy.26
  133.9 5.0 %convolution_convert_fusion = bf16[2048,1024]{1,0:T(8,128)(2,1)S(1)} fusion(bf16[2048,1024]{1,0:T(8,128)(2,1)S(1)} %bitcast.20, bf16[1024,512]{1,0:T(8,128)(2,1)S(1)} %copy-done.4, bf16[1024,512]{1,0:T(8,128)(2,1)S(1)} %copy-done.5), kind=kOutput, calls=%fused_computation.11 | convolution fusion | flops 4301258752 | bytes 10485760 | tf_op jit(solution)/shard_map/dot_general | solution.py:83
  138.9 1.8 fusion.46
  140.8 4.0 %reshape.56 = bf16[8,256,4,128]{3,2,1,0:T(4,128)(2,1)} reshape(bf16[16,128,512]{2,1,0:T(8,128)(2,1)} %get-tuple-element.6) | data formatting | bytes 4194304 | tf_op jit(solution)/shard_map/reshape | solution.py:36
  144.7 2.1 reshape.55
  146.8 4.2 %fusion.47 = (f32[8,4,64]{2,1,0:T(4,128)S(1)}, f32[8,4,64,256]{3,2,1,0:T(8,128)}) fusion(f32[8,256]{1,0:T(8,128)S(1)} %convert_element_type.53, pred[8,256]{1,0:T(8,128)(4,1)S(1)} %gt.23, bf16[8,256,4,128]{3,2,1,0:T(4,128)(2,1)} %reshape.55, bf16[8,64,4,128]{3,2,1,0:T(4,128)(2,1)S(1)} %reshape.49), kind=kOutput, calls=%fused_computation.56 | convolution fusion | flops 136839424 | bytes 4737024 | tf_op jit(solution)/shard_map/sub | solution.py:49
  151.0 2.3 fusion.27
  153.3 0.4 copy.33
  153.7 0.1 copy-done
  153.8 5.6 %fusion.35 = f32[512,4096]{1,0:T(8,128)} fusion(bf16[512,4096]{1,0:T(8,128)(2,1)S(1)} %copy-done, bf16[64,8,4,128]{3,2,1,0:T(4,128)(2,1)S(1)} %bitcast.21), kind=kOutput, calls=%fused_computation.34 | convolution fusion | flops 2147483648 | bytes 13107200 | tf_op jit(solution)/shard_map/dot_general | solution.py:90
  159.4 0.0 reduce-scatter.2.cloned.1.call-update
  159.4 95.3 %reduce-scatter.2.cloned.1.call-done = f32[512,512]{1,0:T(8,128)} async-done(((f32[512,4096]{1,0:T(8,128)}), f32[512,512]{1,0:T(8,128)}) %reduce-scatter.2.cloned.1.call-update) | async-done | bytes 1048592 | tf_op jit(solution)/shard_map/reduce_scatter | solution.py:91
  254.7 2.2 add_convert_fusion
  (20 shorter events, 0.1 us)
Async XLA Ops:
  6.5 56.8 %copy-start.2 = (bf16[512,512]{1,0:T(8,128)(2,1)S(1)}, bf16[512,512]{1,0:T(8,128)(2,1)}, u32[]{:S(2)}) copy-start(bf16[512,512]{1,0:T(8,128)(2,1)} %param.9) | copy-start | bytes 1572868
  6.5 101.1 %all-gather.3.cloned.1.call-start = ((), (), s32[]{:S(2)}) async-start(), calls=%async_computation.1 | async-start | bytes 17825792 | tf_op jit(solution)/shard_map/all_gather | solution.py:71
  7.3 247.5 %reduce-scatter.2.cloned.1.call-start = ((), (), s32[]{:S(2)}) async-start(), calls=%async_computation.2 | async-start | bytes 9437184 | tf_op jit(solution)/shard_map/reduce_scatter | solution.py:91
  7.3 18.3 %collective-permute-start = (bf16[512,512]{1,0:T(8,128)(2,1)}, bf16[512,512]{1,0:T(8,128)(2,1)S(1)}, u32[]{:S(2)}, u32[]{:S(2)}) collective-permute-start(bf16[512,512]{1,0:T(8,128)(2,1)} %param.9), channel_id=1, source_target_pairs={{0,1},{1,2},{2,3},{3,4},{4,5},{5,6},{6,7},{7,0},{8,9},{9,10},{10,1... | collective-permute-start | bytes 1572872 | tf_op jit(solution)/shard_map/ppermute | solution.py:20
  9.8 15.8 %collective-permute-start.1 = (bf16[512,512]{1,0:T(8,128)(2,1)}, bf16[512,512]{1,0:T(8,128)(2,1)S(1)}, u32[]{:S(2)}, u32[]{:S(2)}) collective-permute-start(bf16[512,512]{1,0:T(8,128)(2,1)} %param.9), channel_id=1, source_target_pairs={{0,7},{1,0},{2,1},{3,2},{4,3},{5,4},{6,5},{7,6},{8,15},{9,8},{10,9... | collective-permute-start | bytes 1572872 | tf_op jit(solution)/shard_map/ppermute | solution.py:23
  25.6 13.4 %collective-permute-start.2 = (bf16[512,512]{1,0:T(8,128)(2,1)S(1)}, bf16[512,512]{1,0:T(8,128)(2,1)S(1)}, u32[]{:S(2)}, u32[]{:S(2)}) collective-permute-start(bf16[512,512]{1,0:T(8,128)(2,1)S(1)} %collective-permute-done), channel_id=1, source_target_pairs={{0,1},{1,2},{2,3},{3,4},{4,5},{5,6},{6,7},{7,0},{8,9},{9,10},{10,1... | collective-permute-start | bytes 1572872 | tf_op jit(solution)/shard_map/ppermute | solution.py:20
  25.6 37.8 %collective-permute-start.3 = (bf16[512,512]{1,0:T(8,128)(2,1)S(1)}, bf16[512,512]{1,0:T(8,128)(2,1)S(1)}, u32[]{:S(2)}, u32[]{:S(2)}) collective-permute-start(bf16[512,512]{1,0:T(8,128)(2,1)S(1)} %collective-permute-done.1), channel_id=1, source_target_pairs={{0,7},{1,0},{2,1},{3,2},{4,3},{5,4},{6,5},{7,6},{8,15},{9,8},{10,9... | collective-permute-start | bytes 1572872 | tf_op jit(solution)/shard_map/ppermute | solution.py:23
  39.1 27.5 %collective-permute-start.4 = (bf16[512,512]{1,0:T(8,128)(2,1)S(1)}, bf16[512,512]{1,0:T(8,128)(2,1)S(1)}, u32[]{:S(2)}, u32[]{:S(2)}) collective-permute-start(bf16[512,512]{1,0:T(8,128)(2,1)S(1)} %collective-permute-done.2), channel_id=1, source_target_pairs={{0,1},{1,2},{2,3},{3,4},{4,5},{5,6},{6,7},{7,0},{8,9},{9,10},{10,1... | collective-permute-start | bytes 1572872 | tf_op jit(solution)/shard_map/ppermute | solution.py:20
  63.4 14.1 %collective-permute-start.5 = (bf16[512,512]{1,0:T(8,128)(2,1)S(1)}, bf16[512,512]{1,0:T(8,128)(2,1)S(1)}, u32[]{:S(2)}, u32[]{:S(2)}) collective-permute-start(bf16[512,512]{1,0:T(8,128)(2,1)S(1)} %collective-permute-done.3), channel_id=1, source_target_pairs={{0,7},{1,0},{2,1},{3,2},{4,3},{5,4},{6,5},{7,6},{8,15},{9,8},{10,9... | collective-permute-start | bytes 1572872 | tf_op jit(solution)/shard_map/ppermute | solution.py:23
  66.5 14.8 %collective-permute-start.6 = (bf16[512,512]{1,0:T(8,128)(2,1)S(1)}, bf16[512,512]{1,0:T(8,128)(2,1)S(1)}, u32[]{:S(2)}, u32[]{:S(2)}) collective-permute-start(bf16[512,512]{1,0:T(8,128)(2,1)S(1)} %collective-permute-done.4), channel_id=1, source_target_pairs={{0,1},{1,2},{2,3},{3,4},{4,5},{5,6},{6,7},{7,0},{8,9},{9,10},{10,1... | collective-permute-start | bytes 1572872 | tf_op jit(solution)/shard_map/ppermute | solution.py:20
  67.2 15.1 %copy-start.3 = (bf16[4096,512]{1,0:T(8,128)(2,1)S(1)}, bf16[4096,512]{1,0:T(8,128)(2,1)}, u32[]{:S(2)}) copy-start(bf16[4096,512]{1,0:T(8,128)(2,1)} %param.14) | copy-start | bytes 12582916
  67.2 15.0 %copy-start.6 = (f32[4096]{0:T(1024)S(1)}, f32[4096]{0:T(1024)}, u32[]{:S(2)}) copy-start(f32[4096]{0:T(1024)} %param.10) | copy-start | bytes 49156
  131.4 2.6 copy-start.4
  131.4 2.6 copy-start.5
  146.8 4.2 %copy-start.1 = (bf16[8,256,4,128]{3,2,1,0:T(4,128)(2,1)S(1)}, bf16[8,256,4,128]{3,2,1,0:T(4,128)(2,1)}, u32[]{:S(2)}) copy-start(bf16[8,256,4,128]{3,2,1,0:T(4,128)(2,1)} %reshape.56) | copy-start | bytes 6291460
  151.0 2.8 %copy-start = (bf16[512,4096]{1,0:T(8,128)(2,1)S(1)}, bf16[512,4096]{1,0:T(8,128)(2,1)}, u32[]{:S(2)}) copy-start(bf16[512,4096]{1,0:T(8,128)(2,1)} %param.17) | copy-start | bytes 12582916
Sparse Core Ops, SparseCore 0:
  9.2 98.4 all-gather.2
  159.5 95.1 reduce-scatter.1
